TPU v7x, 32 devices: a whole 2x2x4 slice. The times are simulated.
32 devices in a mesh: groups: 2 (over x), visit: 8 (over z, y), tile: 2 (over core).
Axes of the slice: x: 2, y: 2, z: 4, core: 2. Of those that a mesh axis runs over, the one named last changes fastest.
Arguments:
- exposure: float32 [16, 512, 2048], P(('groups', 'visit'), 'tile'), parts along dimension 0, may hold values from -12 to 12, as said below
- partners: int32 [16, 8], P('groups'), parts along dimension 0, may hold values from 0 to 7, as said below
- offsets: int32 [16, 8], P('groups'), parts along dimension 0, may hold values from -32 to 32
- stamps: int32 [16, 2, 8, 2], P(('groups', 'visit'), 'tile'), parts along dimension 0, may hold values from 0 to 1920, as said below
Outputs:
- difference: float32 [16, 512, 2048], P(('groups', 'visit'), 'tile'), parts along dimension 0
- coefficients: float32 [16, 33], P(('groups', 'visit')), parts along dimension 0
There are 2 independent parts, one for each index of `groups`. A program takes and returns all parts, laid end to end along the dimension named above; each array names one. Nothing has to cross between parts.
Inputs may be any that keep to these rules, and one draw needn't show every extreme that they name: Every row of partners names each of the 8 visits once, and so does every column. `stamps`: A stamp's row anchor lies in 0..128, its column anchor in 0..1920. `exposure`: images of order one.
All inputs are finite; a program needn't handle non-finite values.
Results may differ from a plain program's by a relative error of at most 0.0003.
Values sent between devices are 32-bit elements; how exact they have to be, the bound alone decides.
No kernel may reach another device: no remote copies, remote signals or barrier semaphores. Data moves between devices by JAX's collectives and lax.ppermute only.
A program may use at most 128 MiB of HBM per device.

v0:
```python
import jax
import jax.numpy as jnp
from jax import lax
from jax.sharding import PartitionSpec as P

STAMP = 128
KERNEL = 31
TERMS = 11
SHIFT = 32
RIDGE = 0.05
SIGMA_LIST = (1.0, 1.0, 1.0, 2.0, 2.0, 4.0)
POWER_LIST = (0, 1, 2, 0, 1, 0)
ALL_FILTERS = (0, 1, 2, 3, 4, 5)
COLUMN_PICK = (0, 1, 0, 2, 1, 0, 3, 4, 3, 5)
ROW_PICK = (0, 0, 1, 0, 1, 2, 3, 3, 4, 5)


def extended_2(block, sides, width):
    for axis, dim in sides:
        count = lax.axis_size(axis)
        forward = [(i, i + 1) for i in range(count - 1)]
        backward = [(target, source) for source, target in forward]
        low = lax.ppermute(
            lax.slice_in_dim(block, block.shape[dim] - width, None, axis=dim), axis, forward
        )
        high = lax.ppermute(lax.slice_in_dim(block, 0, width, axis=dim), axis, backward)
        block = jnp.concatenate([low, block, high], axis=dim)
    return block


def profiles():
    taps = (jnp.arange(KERNEL) - KERNEL // 2).astype(jnp.float32)
    stacked = []
    for sigma, power in zip(SIGMA_LIST, POWER_LIST):
        bell = jnp.exp(-taps * taps / (2.0 * sigma * sigma))
        stacked.append(bell * (taps / sigma) ** power / jnp.sum(bell))
    return jnp.stack(stacked)


def coordinates(count, first, total):
    return (
        2.0 * (first + jnp.arange(count, dtype=jnp.int32)).astype(jnp.float32) + 1.0
    ) / total - 1.0


def band(table, picks, count):
    spans = (
        jnp.arange(count + KERNEL - 1, dtype=jnp.int32)[:, None]
        - jnp.arange(count, dtype=jnp.int32)[None, :]
    )
    inside = (spans >= 0) & (spans < KERNEL)
    clipped = jnp.clip(spans, 0, KERNEL - 1)
    chosen = table[jnp.array(picks, dtype=jnp.int32)]
    return jnp.where(inside[None], chosen[:, clipped], 0.0)


def convolve(patch, across, downward):
    spread = jnp.einsum("yq,fqo->yfo", patch, across, precision=lax.Precision.HIGHEST)
    picked = spread[:, jnp.array(COLUMN_PICK, dtype=jnp.int32), :]
    return jnp.einsum("kqy,qkc->kyc", downward, picked, precision=lax.Precision.HIGHEST)


def design_sums(images, science, row_coord, col_coord):
    ones = jnp.ones((row_coord.shape[0], col_coord.shape[0]), jnp.float32)
    poly = jnp.stack([ones, ones * col_coord[None, :], ones * row_coord[:, None]])
    terms = (images[:, None] * poly[None]).reshape(30, -1)
    design = jnp.concatenate([terms, poly.reshape(3, -1)], axis=0)
    gram = jnp.dot(design, design.T, precision=lax.Precision.HIGHEST)
    vector = jnp.dot(design, science.reshape(-1), precision=lax.Precision.HIGHEST)
    return (gram, vector)


def solve_fit(gram, vector):
    regular = gram + RIDGE * jnp.diag(jnp.diag(gram))
    lower = jnp.linalg.cholesky(regular)
    return jax.scipy.linalg.cho_solve((lower, True), vector)


def model_of(images, solution, row_coord, col_coord):
    weights = solution[:30].reshape(10, 3)
    scale = (
        weights[:, 0, None, None]
        + weights[:, 1, None, None] * col_coord[None, None, :]
        + weights[:, 2, None, None] * row_coord[None, :, None]
    )
    background = (
        solution[30] + solution[31] * col_coord[None, :] + solution[32] * row_coord[:, None]
    )
    return jnp.sum(images * scale, axis=0) + background


def shards(exposure, partners, offsets, stamps):
    visits = lax.axis_size("visit")
    tiles = lax.axis_size("tile")
    my_visit = lax.axis_index("visit")
    my_tile = lax.axis_index("tile")
    image = exposure[0]
    height = image.shape[0]
    width = image.shape[1]
    block = height // visits
    blocks = image.reshape(visits, block, width)
    my_sources = lax.dynamic_slice_in_dim(partners, my_visit, 1, 0)[0]
    my_amounts = lax.dynamic_slice_in_dim(offsets, my_visit, 1, 0)[0]
    piece = lax.all_gather(blocks[None], "visit", axis=0, tiled=True)
    owners = jnp.arange(piece.shape[0], dtype=jnp.int32)

    def add_owner(owner_index, total):
        wanted = owners[owner_index] == my_sources
        return total + jnp.where(wanted[:, None, None], piece[owner_index], 0.0)

    assembled = lax.fori_loop(0, piece.shape[0], add_owner, jnp.zeros_like(blocks))
    padded_cols = jnp.pad(assembled, ((0, 0), (0, 0), (SHIFT, SHIFT)))

    def shift_block(rows_block, amount):
        return lax.dynamic_slice_in_dim(rows_block, SHIFT + amount, width, 1)

    template = jax.vmap(shift_block)(padded_cols, my_amounts).reshape(height, width)
    half = KERNEL // 2
    extended = extended_2(template, (("tile", 0),), half)
    field = jnp.pad(extended, ((0, 0), (half, half)))
    table = profiles()
    row_coord = coordinates(height, my_tile * height, height * tiles)
    col_coord = coordinates(width, 0, width)
    stamp_across = band(table, ALL_FILTERS, STAMP)
    stamp_down = band(table, ROW_PICK, STAMP)

    def add_stamp(carry, anchor):
        row_start = anchor[0]
        col_start = anchor[1]
        patch = lax.dynamic_slice(
            field, (row_start, col_start), (STAMP + 2 * half, STAMP + 2 * half)
        )
        images = convolve(patch, stamp_across, stamp_down)
        science_cut = lax.dynamic_slice(image, (row_start, col_start), (STAMP, STAMP))
        row_part = lax.dynamic_slice_in_dim(row_coord, row_start, STAMP)
        col_part = lax.dynamic_slice_in_dim(col_coord, col_start, STAMP)
        gram_term, vector_term = design_sums(images, science_cut, row_part, col_part)
        return ((carry[0] + gram_term, carry[1] + vector_term), None)

    start = (jnp.zeros((3 * TERMS, 3 * TERMS), jnp.float32), jnp.zeros((3 * TERMS,), jnp.float32))
    (gram, vector), _ = lax.scan(add_stamp, start, stamps[0, 0])
    gram, vector = lax.psum((gram, vector), "tile")
    solution = solve_fit(gram, vector)
    across = band(table, ALL_FILTERS, 128)
    row_blocks = height // STAMP
    col_blocks = width // 128

    def image_block(block_index):
        row_start = block_index // col_blocks * STAMP
        col_start = block_index % col_blocks * 128
        patch = lax.dynamic_slice(field, (row_start, col_start), (STAMP + 2 * half, 128 + 2 * half))
        images = convolve(patch, across, stamp_down)
        row_part = lax.dynamic_slice_in_dim(row_coord, row_start, STAMP)
        col_part = lax.dynamic_slice_in_dim(col_coord, col_start, 128)
        science_cut = lax.dynamic_slice(image, (row_start, col_start), (STAMP, 128))
        return science_cut - model_of(images, solution, row_part, col_part)

    pieces = lax.map(image_block, jnp.arange(row_blocks * col_blocks, dtype=jnp.int32))
    pieces = pieces.reshape(row_blocks, col_blocks, STAMP, 128)
    difference = jnp.transpose(pieces, (0, 2, 1, 3)).reshape(height, width)
    return (difference[None], solution[None])


def solution(mesh):
    return jax.shard_map(
        shards,
        mesh=mesh,
        in_specs=(
            P(("groups", "visit"), "tile", None),
            P("groups", None),
            P("groups", None),
            P(("groups", "visit"), "tile", None, None),
        ),
        out_specs=(P(("groups", "visit"), "tile", None), P(("groups", "visit"), None)),
        check_vma=False,
    )
```

profile of v0, /device:TPU:0, one launch (start us, length us, event | category | flops | bytes accessed | tf_op | source)
XLA Modules:
  0.0 918.3 jit_solution(15050697580024253793)
XLA Ops:
  13.1 37.8 %gather_fusion.5 = f32[20224,10]{1,0:T(8,128)} fusion(f32[10,31]{0,1:T(8,128)S(1)} %copy.28, s32[20480]{0:T(1024)S(1)} %pad_clamp_fusion.2), kind=kCustom, calls=%fused_computation.5 | custom fusion | bytes 1698816 | tf_op jit(solution)/shard_map/gather | solution.py:54
  50.9 6.8 copy.29
  58.4 37.8 %gather_fusion.3 = f32[20224,6]{1,0:T(8,128)} fusion(f32[6,31]{0,1:T(8,128)S(1)} %copy.26, s32[20480]{0:T(1024)S(1)} %pad_clamp_fusion.2), kind=kCustom, calls=%fused_computation.3 | custom fusion | bytes 1051648 | tf_op jit(solution)/shard_map/gather | solution.py:54
  96.2 7.2 copy.27
  105.4 135.1 %all-gather.2.cloned.1.call-done = f32[8,8,32,2048]{3,2,1,0:T(8,128)} async-done(((f32[1,8,32,2048]{3,2,1,0:T(8,128)}), f32[8,8,32,2048]{3,2,1,0:T(8,128)}) %all-gather.2.cloned.1.call-update) | async-done | bytes 16777232 | tf_op jit(solution)/shard_map/all_gather | solution.py:104
  240.5 27.8 %while.44 = (s32[]{:T(128)}, f32[8,32,2048]{2,1,0:T(8,128)S(1)}, s32[8]{0:T(128)S(1)}, s32[8]{0:T(128)S(1)}, f32[8,8,32,2048]{3,2,1,0:T(8,128)}, /*index=5*/s32[]{:T(128)}, s32[]{:T(128)}) while((s32[]{:T(128)}, f32[8,32,2048]{2,1,0:T(8,128)S(1)}, s32[8]{0:T(128)S(1)}, s32[8]{0:T(128)S(1)}, f32[8,8,32,2048]{3,2,1,0:T(8,128)}, ...), condition=%wide.region_1.2_spmd.clone, body=%wide.region_0.1_spmd.clone.sunk | while | flops 1572875 | bytes 6291611 | solution.py:111
  270.4 30.2 %while.42 = (s32[]{:T(128)}, f32[8,32,2112]{2,1,0:T(8,128)}, s32[8,3]{0,1:T(4,128)S(1)}, f32[8,32,2048]{2,1,0:T(8,128)}, s32[]{:T(128)}) while((s32[]{:T(128)}, f32[8,32,2112]{2,1,0:T(8,128)}, s32[8,3]{0,1:T(4,128)S(1)}, f32[8,32,2048]{2,1,0:T(8,128)}, s32[]{:T(128)}) %tuple.124), condition=%wide.while_cond, body=%wide.while_body.sunk | while | flops 2 | bytes 525929 | solution.py:115
  271.0 3.1 dynamic-slice_dynamic-update-slice_fusion.2
  274.8 3.1 dynamic-slice_dynamic-update-slice_fusion.2
  278.6 3.1 dynamic-slice_dynamic-update-slice_fusion.2
  282.4 3.1 dynamic-slice_dynamic-update-slice_fusion.2
  286.1 3.1 dynamic-slice_dynamic-update-slice_fusion.2
  306.2 3.8 select_maximum_fusion
  310.0 177.0 %while.45 = (s32[]{:T(128)}, f32[33,33]{1,0:T(8,128)S(1)}, f32[33]{0:T(128)S(1)}, s32[8,2]{0,1:T(2,128)S(1)}, f32[286,2078]{1,0:T(8,128)}, /*index=5*/f32[6,158,...) while((s32[]{:T(128)}, f32[33,33]{1,0:T(8,128)S(1)}, ...), condition=%wide.region_6.7_spmd.clone.clone, body=%wide.region_5.6_spmd.sunk.clone.clone.sunk | while | flops 762977472 | bytes 24572200 | solution.py:141
  326.5 3.2 fusion.75
  348.6 3.2 fusion.75
  370.8 3.2 fusion.75
  392.9 3.2 fusion.75
  415.0 3.2 fusion.75
  437.2 3.2 fusion.75
  459.3 3.2 fusion.75
  481.4 3.2 fusion.75
  486.9 3.7 all-reduce.3
  499.2 408.5 %while.43 = (s32[]{:T(128)}, f32[32,128,128]{1,2,0:T(8,128)}, s32[32]{0:T(128)S(1)}, f32[256,2048]{1,0:T(8,128)}, f32[286,2078]{1,0:T(8,128)}, /*index=5*/f32[6,...) while((s32[]{:T(128)}, f32[32,128,128]{1,2,0:T(8,128)}, ...), condition=%wide.region_13.14_spmd.clone, body=%wide.region_11.13_spmd.sunk.clone.sunk | while | flops 541238400 | bytes 4926202 | solution.py:158
  (741 shorter events, 484.5 us)
Async XLA Ops:
  7.2 96.2 %copy-start = (s32[8,8]{1,0:T(8,128)S(1)}, s32[8,8]{1,0:T(8,128)}, u32[]{:S(2)}) copy-start(s32[8,8]{1,0:T(8,128)} %param.16) | copy-start | bytes 772
  7.2 5.2 copy-start.7
  7.2 233.3 %all-gather.2.cloned.1.call-start = ((), (), s32[]{:S(2)}) async-start(), calls=%async_computation | async-start | bytes 18874368 | tf_op jit(solution)/shard_map/all_gather | solution.py:104
  301.6 2.9 collective-permute-start
  302.9 3.2 collective-permute-start.1
  304.4 5.5 copy-start.5
  304.5 5.5 copy-start.6
  323.5 1.2 copy-start.3
  326.5 3.2 copy-start.2
  345.5 1.2 copy-start.3
  348.6 3.2 copy-start.2
  367.7 1.2 copy-start.3
  370.7 3.2 copy-start.2
  389.8 1.2 copy-start.3
  392.9 3.2 copy-start.2
  411.9 1.2 copy-start.3
  415.0 3.2 copy-start.2
  434.1 1.2 copy-start.3
  437.1 3.2 copy-start.2
  456.2 1.2 copy-start.3
  459.3 3.2 copy-start.2
  481.4 3.2 copy-start.2
  907.7 2.3 copy-start.4
  910.0 1.5 copy-start.1
  (1 other events, 1.2 us)
Sparse Core Ops, SparseCore 0:
  10.2 230.3 all-gather.1
where the time goes:
time: 925 us; the launch traced here: 918 us
  local copies, waits for them, and re-layouts  275 us (30%)
  matrix products  198 us (21%)
  loops' own time  146 us (16%)
  other arithmetic  141 us (15%)
  waiting for transfers between devices  137 us (15%)
  between operations  14.3 us (2%)
    all_gather x1, waiting for transfers between devices, shards(): piece = lax.all_gather(blocks[None], 'visit', axis=0, tiled=True)  135 us
    dot_general x40, matrix products, convolve(): jnp.einsum('kqy,qkc->kyc', downward, picked, precision=lax.Precision.HIGH...  92 us
    another operation x1, loops' own time, shards(): lax.map(image_block, jnp.arange(row_blocks * col_blocks, dtype=jnp.int32))  91.6 us
    gather x4, local copies, waits for them, and re-layouts, band(): return jnp.where(inside[None], chosen[:, clipped], 0.0)  89.5 us
    add x32, other arithmetic, model_of(): solution[30] + solution[31] * col_coord[None, :]  65 us
    dot_general x40, matrix products, convolve(): jnp.einsum('yq,fqo->yfo', patch, across, precision=lax.Precision.HIGHEST)  62.2 us
    another operation x1, loops' own time, shards(): (gram, vector), _ = lax.scan(add_stamp, start, stamps[0, 0])  54 us
    gather x24, local copies, waits for them, and re-layouts  30.2 us
  transfers between devices with their start and end apart: 3, of which 2 were waited for; matrix products, arithmetic and copies ran while one was open for 11% of the time, Pallas kernels for 0%

commit v1 on v0

--- a/solution.py
+++ b/solution.py
@@ -101,7 +101,15 @@
     blocks = image.reshape(visits, block, width)
     my_sources = lax.dynamic_slice_in_dim(partners, my_visit, 1, 0)[0]
     my_amounts = lax.dynamic_slice_in_dim(offsets, my_visit, 1, 0)[0]
-    piece = lax.all_gather(blocks[None], "visit", axis=0, tiled=True)
+    ways, here, hop = (lax.axis_size("visit"), lax.axis_index("visit"), blocks[None].shape[0])
+    line, have = (blocks[None], 1)
+    while have < ways:
+        line = jnp.concatenate(
+            [line, lax.ppermute(line, "visit", [(d, (d - have) % ways) for d in range(ways)])],
+            axis=0,
+        )
+        have = 2 * have
+    piece = jnp.roll(line, here * hop, axis=0)
     owners = jnp.arange(piece.shape[0], dtype=jnp.int32)
 
     def add_owner(owner_index, total):

time: 925 us -> 1210 us (1.31)
  waiting for transfers between devices: 137 us -> 394 us
  local copies, waits for them, and re-layouts: 275 us -> 309 us
  loops' own time: 146 us -> 128 us
  between operations: 14.3 us -> 0.93 us
    ppermute x0 -> x3, waiting for transfers between devices: none -> 392 us  [shards(): lax.ppermute(line, 'visit', [(d, (d - have) % ways) for d in range(ways)])]
    all_gather x1 -> x0, waiting for transfers between devices: 135 us -> none  [shards(): piece = lax.all_gather(blocks[None], 'visit', axis=0, tiled=True)]
    unnamed x13 -> x32, local copies, waits for them, and re-layouts: 0.04 us -> 21.1 us
    another operation x1, loops' own time: 91.6 us -> 76.1 us  [shards(): lax.map(image_block, jnp.arange(row_blocks * col_blocks, dtype=jnp.int32))]
  transfers between devices with their start and end apart: 3 -> 5, of which waited for: 2 -> 4; matrix products, arithmetic and copies ran while one was open for 11% -> 8% of each run, Pallas kernels for 0% -> 0%
where the time goes in v1:
time: 1210 us; the launch traced here: 1200 us
  waiting for transfers between devices  394 us (33%)
  local copies, waits for them, and re-layouts  309 us (26%)
  matrix products  208 us (17%)
  other arithmetic  145 us (12%)
  loops' own time  128 us (11%)
    ppermute x3, waiting for transfers between devices, shards(): lax.ppermute(line, 'visit', [(d, (d - have) % ways) for d in range(ways)])  392 us
    dot_general x40, matrix products, convolve(): jnp.einsum('kqy,qkc->kyc', downward, picked, precision=lax.Precision.HIGH...  92 us
    gather x4, local copies, waits for them, and re-layouts, band(): return jnp.where(inside[None], chosen[:, clipped], 0.0)  88.7 us
    another operation x1, loops' own time, shards(): lax.map(image_block, jnp.arange(row_blocks * col_blocks, dtype=jnp.int32))  76.1 us
    add x32, other arithmetic, model_of(): solution[30] + solution[31] * col_coord[None, :]  62.3 us
    dot_general x40, matrix products, convolve(): jnp.einsum('yq,fqo->yfo', patch, across, precision=lax.Precision.HIGHEST)  62.2 us
    another operation x1, loops' own time, shards(): (gram, vector), _ = lax.scan(add_stamp, start, stamps[0, 0])  51.6 us
    dynamic_slice x64, local copies, waits for them, and re-layouts, image_block(): science_cut = lax.dynamic_slice(image, (row_start, col_start), (STAMP, 128))  30.1 us
  transfers between devices with their start and end apart: 5, of which 4 were waited for; matrix products, arithmetic and copies ran while one was open for 8% of the time, Pallas kernels for 0%

profile of v1, /device:TPU:0, one launch (start us, length us, event | category | flops | bytes accessed | tf_op | source)
XLA Modules:
  0.0 1198.8 jit_solution(15404687086128279034)
XLA Ops:
  0.7 6.1 collective-permute-start
  6.7 45.2 %collective-permute-done = f32[1,8,32,2048]{3,2,1,0:T(8,128)S(1)} collective-permute-done((f32[1,8,32,2048]{3,2,1,0:T(8,128)}, f32[1,8,32,2048]{3,2,1,0:T(8,128)S(1)}, u32[]{:S(2)}, u32[]{:S(2)}) %collective-permute-start) | collective-permute-done | bytes 2097184 | tf_op jit(solution)/shard_map/ppermute | solution.py:108
  56.3 90.0 %collective-permute-done.1 = f32[2,8,32,2048]{3,2,1,0:T(8,128)S(1)} collective-permute-done((f32[2,8,32,2048]{3,2,1,0:T(8,128)S(1)}, f32[2,8,32,2048]{3,2,1,0:T(8,128)S(1)}, u32[]{:S(2)}, u32[]{:S(2)}) %collective-permute-start.1) | collective-permute-done | bytes 4194336 | tf_op jit(solution)/shard_map/ppermute | solution.py:108
  146.3 3.9 pad_maximum_fusion.10
  156.4 38.0 %gather_fusion.5 = f32[20224,10]{1,0:T(8,128)} fusion(f32[10,31]{0,1:T(8,128)S(1)} %copy.28, s32[20480]{0:T(1024)S(1)} %pad_clamp_fusion.2), kind=kCustom, calls=%fused_computation.5 | custom fusion | bytes 1698816 | tf_op jit(solution)/shard_map/gather | solution.py:54
  194.4 6.8 copy.29
  201.8 38.0 %gather_fusion.3 = f32[20224,6]{1,0:T(8,128)} fusion(f32[6,31]{0,1:T(8,128)S(1)} %copy.26, s32[20480]{0:T(1024)S(1)} %pad_clamp_fusion.2), kind=kCustom, calls=%fused_computation.3 | custom fusion | bytes 1051648 | tf_op jit(solution)/shard_map/gather | solution.py:54
  239.8 6.0 copy.27
  255.3 256.9 %collective-permute-done.2 = f32[4,8,32,2048]{3,2,1,0:T(8,128)} collective-permute-done((f32[4,8,32,2048]{3,2,1,0:T(8,128)}, f32[4,8,32,2048]{3,2,1,0:T(8,128)}, u32[]{:S(2)}, u32[]{:S(2)}) %collective-permute-start.2) | collective-permute-done | bytes 8388640 | tf_op jit(solution)/shard_map/ppermute | solution.py:108
  512.2 7.7 constant_dynamic-update-slice_fusion.4
  525.1 7.7 constant_dynamic-update-slice_fusion
  532.8 11.8 constant_dynamic-slice_fusion.3
  544.6 27.8 %while.44 = (s32[]{:T(128)}, f32[8,32,2048]{2,1,0:T(8,128)S(1)}, s32[8]{0:T(128)S(1)}, s32[8]{0:T(128)S(1)}, f32[8,8,32,2048]{3,2,1,0:T(8,128)}, /*index=5*/s32[]{:T(128)}, s32[]{:T(128)}) while((s32[]{:T(128)}, f32[8,32,2048]{2,1,0:T(8,128)S(1)}, s32[8]{0:T(128)S(1)}, s32[8]{0:T(128)S(1)}, f32[8,8,32,2048]{3,2,1,0:T(8,128)}, ...), condition=%wide.region_1.2_spmd.clone, body=%wide.region_0.1_spmd.clone.sunk | while | flops 1572875 | bytes 6291611 | solution.py:119
  574.4 28.7 %while.42 = (s32[]{:T(128)}, f32[8,32,2112]{2,1,0:T(8,128)}, s32[8,3]{0,1:T(4,128)S(1)}, f32[8,32,2048]{2,1,0:T(8,128)}, s32[]{:T(128)}) while((s32[]{:T(128)}, f32[8,32,2112]{2,1,0:T(8,128)}, s32[8,3]{0,1:T(4,128)S(1)}, f32[8,32,2048]{2,1,0:T(8,128)}, s32[]{:T(128)}) %tuple.125), condition=%wide.while_cond, body=%wide.while_body.sunk | while | flops 2 | bytes 525929 | solution.py:123
  608.7 3.8 select_maximum_fusion
  612.5 183.6 %while.45 = (s32[]{:T(128)}, f32[33,33]{1,0:T(8,128)S(1)}, f32[33]{0:T(128)S(1)}, s32[8,2]{0,1:T(2,128)S(1)}, f32[286,2078]{1,0:T(8,128)}, /*index=5*/f32[6,158,...) while((s32[]{:T(128)}, f32[33,33]{1,0:T(8,128)S(1)}, ...), condition=%wide.region_6.7_spmd.clone.clone, body=%wide.region_5.6_spmd.sunk.clone.clone.sunk | while | flops 762977472 | bytes 23785740 | solution.py:149
  631.8 3.5 fusion.75
  654.8 3.5 fusion.75
  677.8 3.5 fusion.75
  700.7 3.5 fusion.75
  723.7 3.5 fusion.75
  769.6 3.5 fusion.75
  796.0 3.7 all-reduce.3
  808.0 387.0 %while.43 = (s32[]{:T(128)}, f32[32,128,128]{1,2,0:T(8,128)}, s32[32]{0:T(128)S(1)}, f32[256,2048]{1,0:T(8,128)}, f32[286,2078]{1,0:T(8,128)}, /*index=5*/f32[6,...) while((s32[]{:T(128)}, f32[32,128,128]{1,2,0:T(8,128)}, ...), condition=%wide.region_13.14_spmd.clone, body=%wide.region_11.13_spmd.sunk.clone.sunk | while | flops 541238400 | bytes 4926202 | solution.py:166
  (750 shorter events, 523.7 us)
Async XLA Ops:
  0.6 245.1 %copy-start = (s32[8,8]{1,0:T(8,128)S(1)}, s32[8,8]{1,0:T(8,128)}, u32[]{:S(2)}) copy-start(s32[8,8]{1,0:T(8,128)} %param.16) | copy-start | bytes 772
  0.6 145.6 %copy-start.3 = (f32[1,256,2048]{2,1,0:T(8,128)S(1)}, f32[1,256,2048]{2,1,0:T(8,128)}, u32[]{:S(2)}) copy-start(f32[1,256,2048]{2,1,0:T(8,128)} %param.15) | copy-start | bytes 6291460
  0.7 51.3 %collective-permute-start = (f32[1,8,32,2048]{3,2,1,0:T(8,128)}, f32[1,8,32,2048]{3,2,1,0:T(8,128)S(1)}, u32[]{:S(2)}, u32[]{:S(2)}) collective-permute-start(f32[1,8,32,2048]{3,2,1,0:T(8,128)} %bitcast.165), channel_id=1, source_target_pairs={{0,14},{2,0},{4,2},{6,4},{8,6},{10,8},{12,10},{14,12},{1,15},{3,1}... | collective-permute-start | bytes 6291464 | tf_op jit(solution)/shard_map/ppermute | solution.py:108
  51.9 94.4 %copy-start.6 = (f32[1,8,32,2048]{3,2,1,0:T(8,128)}, f32[1,8,32,2048]{3,2,1,0:T(8,128)S(1)}, u32[]{:S(2)}) copy-start(f32[1,8,32,2048]{3,2,1,0:T(8,128)S(1)} %collective-permute-done) | copy-start | bytes 6291460
  54.8 100.9 %copy-start.12 = (s32[10]{0:T(128)S(1)}, s32[10]{0:T(128)}, u32[]{:S(2)}) copy-start(s32[10]{0:T(128)} %constant.340) | copy-start | bytes 124
  54.8 91.5 %collective-permute-start.1 = (f32[2,8,32,2048]{3,2,1,0:T(8,128)S(1)}, f32[2,8,32,2048]{3,2,1,0:T(8,128)S(1)}, u32[]{:S(2)}, u32[]{:S(2)}) collective-permute-start(f32[2,8,32,2048]{3,2,1,0:T(8,128)S(1)} %pad_maximum_fusion.11), channel_id=1, source_target_pairs={{0,12},{2,14},{4,0},{6,2},{8,4},{10,6},{12,8},{14,10},{1,13},{3,15... | collective-permute-start | bytes 12582920 | tf_op jit(solution)/shard_map/ppermute | solution.py:108
  146.3 4.6 copy-start.4
  150.9 361.4 %collective-permute-start.2 = (f32[4,8,32,2048]{3,2,1,0:T(8,128)}, f32[4,8,32,2048]{3,2,1,0:T(8,128)}, u32[]{:S(2)}, u32[]{:S(2)}) collective-permute-start(f32[4,8,32,2048]{3,2,1,0:T(8,128)} %pad_maximum_fusion.10), channel_id=1, source_target_pairs={{0,8},{2,10},{4,12},{6,14},{8,0},{10,2},{12,4},{14,6},{1,9},{3,11}... | collective-permute-start | bytes 25165832 | tf_op jit(solution)/shard_map/ppermute | solution.py:108
  247.8 2.3 copy-start.7
  250.2 2.9 copy-start.5
  532.8 11.8 copy-start.2
  604.1 8.4 copy-start.10
  604.1 8.4 copy-start.11
  604.1 2.8 collective-permute-start.3
  605.4 3.2 collective-permute-start.4
  625.7 1.2 copy-start.8
  648.6 1.2 copy-start.8
  671.5 1.2 copy-start.8
  694.5 1.2 copy-start.8
  717.4 1.2 copy-start.8
  740.4 1.2 copy-start.8
  763.4 1.2 copy-start.8
  1195.0 3.8 copy-start.9
  1195.0 3.8 copy-start.1
  (1 other events, 1.2 us)
